TPU v7x, 256 devices: a whole 4x4x8 slice. The times are simulated.
256 devices in a mesh: dp: 32 (over x, y, core), expert: 8 (over z).
Axes of the slice: x: 4, y: 4, z: 8, core: 2. Of those that a mesh axis runs over, the one named last changes fastest.
Arguments:
- tokens: bfloat16 [32768, 2048], P(('dp', 'expert')), may hold values from -6 to 6
- expert_ids: int32 [32768, 3], P(('dp', 'expert')), may hold values from 0 to 7, as said below
- slot_index: int32 [32768, 3], P(('dp', 'expert')), may hold values from -1 to 47, as said below
- w_router: float32 [2048, 8], replicated, may hold values from -0.125 to 0.125
- w_gate: bfloat16 [8, 2048, 768], P('expert'), may hold values from -0.125 to 0.125
- w_up: bfloat16 [8, 2048, 768], P('expert'), may hold values from -0.125 to 0.125
- w_down: bfloat16 [8, 2048, 768], P('expert'), may hold values from -0.21875 to 0.21875
- grad_out: bfloat16 [32768, 2048], P(('dp', 'expert')), may hold values from -0.59765625 to 0.59765625
Outputs:
- layer_output: bfloat16 [32768, 2048], P(('dp', 'expert'))
- grad_tokens: bfloat16 [32768, 2048], P(('dp', 'expert'))
- grad_router: float32 [2048, 8], replicated
- grad_gate: float32 [8, 2048, 768], P('expert', 'dp')
- grad_up: float32 [8, 2048, 768], P('expert', 'dp')
- grad_down: float32 [8, 2048, 768], P('expert', 'dp')
Inputs may be any that keep to these rules, and one draw needn't show every extreme that they name: `expert_ids`: each token names 3 different experts. `slot_index`: the live choices of one device's 128 tokens to one expert take the slots 0, 1, 2, ... in the order of tokens and then choices, and choices past 48 of them get -1; in every draw some expert gets all 48 slots from every device.
All inputs are finite; a program needn't handle non-finite values.
Results may differ from a plain program's by a relative error of at most 0.025.
Values may be sent and summed in bfloat16 or wider, within the bound.
No kernel may reach another device: no remote copies, remote signals or barrier semaphores. Data moves between devices by JAX's collectives and lax.ppermute only.
A program may use at most 128 MiB of HBM per device.

v0:
```python
import jax
import jax.numpy as jnp
from jax import lax
from jax.sharding import PartitionSpec as P


def silu_parts(hidden):
    sigmoid_val = jax.nn.sigmoid(hidden)
    return (hidden * sigmoid_val, sigmoid_val * (1.0 + hidden * (1.0 - sigmoid_val)))


def on_device(tokens, expert_ids, slot_index, w_router, w_gate, w_up, w_down, grad_out):
    tok_count, width = tokens.shape
    choice_count = expert_ids.shape[1]
    expert_count = w_router.shape[1]
    local_count = w_gate.shape[0]
    hidden_width = w_gate.shape[2]
    sender_count = lax.axis_size("expert")
    own_rows = width // lax.axis_size("dp")
    slot_count = tok_count * choice_count // expert_count
    highest = lax.Precision.HIGHEST
    tokens_wide = tokens.astype(jnp.float32)
    scores = jax.nn.sigmoid(jnp.dot(tokens_wide, w_router, precision=highest))
    picker = (
        expert_ids[:, :, None] == jnp.arange(expert_count, dtype=jnp.int32)[None, None, :]
    ).astype(jnp.float32)
    picked = jnp.sum(picker * scores[:, None, :], axis=2)
    pick_sum = jnp.sum(picked, axis=1, keepdims=True)
    gate_value = picked / pick_sum
    is_live = slot_index >= 0
    live_gate = jnp.where(is_live, gate_value, 0.0)
    position = jnp.where(is_live, expert_ids * slot_count + slot_index, expert_count * slot_count)
    owner_table = jnp.full((expert_count * slot_count + 1,), tok_count * choice_count, jnp.int32)
    owner_table = owner_table.at[position.reshape(-1)].set(
        jnp.arange(tok_count * choice_count, dtype=jnp.int32)
    )
    owner_table = owner_table[: expert_count * slot_count]
    zero_row = jnp.zeros((1, width), jnp.bfloat16)
    token_pad = jnp.concatenate([tokens, zero_row], axis=0)
    outgoing = token_pad[owner_table // choice_count].reshape(expert_count, slot_count, width)
    received = lax.all_to_all(outgoing, "expert", split_axis=0, concat_axis=0, tiled=True)
    item_count = received.shape[1]
    expert_row_block = received.reshape(sender_count, local_count, item_count, width)
    hidden_gate = jnp.einsum(
        "slnd,ldf->slnf", expert_row_block, w_gate, preferred_element_type=jnp.float32
    )
    hidden_up = jnp.einsum(
        "slnd,ldf->slnf", expert_row_block, w_up, preferred_element_type=jnp.float32
    )
    expert_activated = (silu_parts(hidden_gate)[0] * hidden_up).astype(jnp.bfloat16)
    expert_out = jnp.einsum(
        "slnf,ldf->slnd", expert_activated, w_down, preferred_element_type=jnp.float32
    ).astype(jnp.bfloat16)
    returned = lax.all_to_all(
        expert_out.reshape(sender_count * local_count, item_count, width),
        "expert",
        split_axis=0,
        concat_axis=0,
        tiled=True,
    )
    flat_shape = (sender_count * local_count, item_count, hidden_width)
    results = (
        returned,
        received,
        hidden_gate.reshape(flat_shape),
        hidden_up.reshape(flat_shape),
        expert_activated.reshape(flat_shape),
    )
    returned = results[0]
    received = results[1]
    out_pad = jnp.concatenate([returned.reshape(-1, width), zero_row], axis=0)
    dy_wide = grad_out.astype(jnp.float32)
    mixed = jnp.zeros((tok_count, width), jnp.float32)
    gate_grads = []
    for which in range(choice_count):
        got_row = out_pad[position[:, which]].astype(jnp.float32)
        mixed = mixed + live_gate[:, which : which + 1] * got_row
        gate_grads.append(jnp.sum(dy_wide * got_row, axis=1))
    layer_output = mixed.astype(jnp.bfloat16)
    gate_grad = jnp.stack(gate_grads, axis=1)
    gate_pad = jnp.concatenate([live_gate.reshape(-1), jnp.zeros((1,), jnp.float32)])
    grad_pad = jnp.concatenate([grad_out, zero_row], axis=0)
    grad_rows = (
        gate_pad[owner_table][:, None] * grad_pad[owner_table // choice_count].astype(jnp.float32)
    ).astype(jnp.bfloat16)
    grad_rows = grad_rows.reshape(expert_count, slot_count, width)
    block_shape = (sender_count, local_count, slot_count, width)
    arrived = lax.all_to_all(grad_rows, "expert", split_axis=0, concat_axis=0, tiled=True).reshape(
        block_shape
    )
    row_block = received.reshape(block_shape)
    hidden_shape = (sender_count, local_count, slot_count, hidden_width)
    hidden_gate = results[2].reshape(hidden_shape)
    hidden_up = results[3].reshape(hidden_shape)
    activated = results[4].reshape(hidden_shape)
    silu_value, silu_slope = silu_parts(hidden_gate)
    grad_act = jnp.einsum("slnd,ldf->slnf", arrived, w_down, preferred_element_type=jnp.float32)
    gate_delta = (grad_act * hidden_up * silu_slope).astype(jnp.bfloat16)
    up_delta = (grad_act * silu_value).astype(jnp.bfloat16)
    row_grad = (
        jnp.einsum("slnf,ldf->slnd", gate_delta, w_gate, preferred_element_type=jnp.float32)
        + jnp.einsum("slnf,ldf->slnd", up_delta, w_up, preferred_element_type=jnp.float32)
    ).astype(jnp.bfloat16)
    sent_back = lax.all_to_all(
        row_grad.reshape(sender_count * local_count, slot_count, width),
        "expert",
        split_axis=0,
        concat_axis=0,
        tiled=True,
    )
    piece = row_block
    gate_part = jnp.einsum("slnd,slnf->dlf", piece, gate_delta, preferred_element_type=jnp.float32)
    up_part = jnp.einsum("slnd,slnf->dlf", piece, up_delta, preferred_element_type=jnp.float32)
    gate_part, up_part = (gate_part, up_part)
    piece = arrived
    down_part = (
        jnp.einsum("slnd,slnf->dlf", piece, activated, preferred_element_type=jnp.float32)
        .reshape(lax.axis_size("dp") * own_rows, local_count * hidden_width)
        .reshape(lax.axis_size("dp") * own_rows, local_count, hidden_width)
    )
    joined = lax.psum_scatter(
        jnp.concatenate([gate_part, up_part, down_part], axis=2)
        .reshape(lax.axis_size("dp") * own_rows, local_count * 3 * hidden_width)
        .astype(jnp.bfloat16),
        "dp",
        scatter_dimension=0,
        tiled=True,
    ).astype(jnp.float32)
    triple_view = joined.reshape(-1, local_count, 3, hidden_width)
    grad_gate = jnp.transpose(triple_view[:, :, 0, :], (1, 0, 2))
    grad_up = jnp.transpose(triple_view[:, :, 1, :], (1, 0, 2))
    grad_down = jnp.transpose(triple_view[:, :, 2, :], (1, 0, 2))
    back_pad = jnp.concatenate([sent_back.reshape(-1, width), zero_row], axis=0)
    row_sum = jnp.zeros((tok_count, width), jnp.float32)
    for which in range(choice_count):
        row_sum = row_sum + back_pad[position[:, which]].astype(jnp.float32)
    cross_term = jnp.sum(gate_grad * gate_value, axis=1, keepdims=True)
    pick_delta = (gate_grad - cross_term) / pick_sum * picked * (1.0 - picked)
    logit_grad = jnp.sum(picker * pick_delta[:, :, None], axis=1)
    grad_tokens = (row_sum + jnp.dot(logit_grad, w_router.T, precision=highest)).astype(
        jnp.bfloat16
    )
    grad_router = lax.psum(jnp.dot(tokens_wide.T, logit_grad, precision=highest), ("dp", "expert"))
    return (layer_output, grad_tokens, grad_router, grad_gate, grad_up, grad_down)


def solution(mesh):
    return jax.shard_map(
        on_device,
        mesh=mesh,
        in_specs=(
            P(("dp", "expert"), None),
            P(("dp", "expert"), None),
            P(("dp", "expert"), None),
            P(),
            P("expert", None, None),
            P("expert", None, None),
            P("expert", None, None),
            P(("dp", "expert"), None),
        ),
        out_specs=(
            P(("dp", "expert"), None),
            P(("dp", "expert"), None),
            P(),
            P("expert", "dp", None),
            P("expert", "dp", None),
            P("expert", "dp", None),
        ),
        check_vma=False,
    )
```

profile of v0, /device:TPU:1, one launch (start us, length us, event | category | flops | bytes accessed | tf_op | source)
XLA Modules:
  0.0 503.2 jit_solution(17069465970971020080)
XLA Ops:
  9.2 2.9 scatter_custom_fusion
  14.1 6.2 %gather_fusion = bf16[384,2048]{1,0:T(8,128)(2,1)} fusion(bf16[129,2048]{1,0:T(8,128)(2,1)} %concatenate.23, s32[1024]{0:T(1024)S(1)} %get-tuple-element.27), kind=kCustom, calls=%fused_computation | custom fusion | bytes 3147264 | tf_op jit(solution)/shard_map/gather | solution.py:40
  20.3 9.0 %all-to-all-start = ((bf16[8,48,2048]{2,1,0:T(8,128)(2,1)}), bf16[8,48,2048]{2,1,0:T(8,128)(2,1)}, u32[]{:S(2)}, u32[]{:S(2)}) async-start(bf16[8,48,2048]{2,1,0:T(8,128)(2,1)} %bitcast.129), calls=%async_computation | async-start | bytes 3145728 | tf_op jit(solution)/shard_map/all_to_all | solution.py:41
  31.2 6.2 %gather_fusion.5 = bf16[384,2048]{1,0:T(8,128)(2,1)} fusion(bf16[129,2048]{1,0:T(8,128)(2,1)} %concatenate.26, s32[1024]{0:T(1024)S(1)} %get-tuple-element.27), kind=kCustom, calls=%fused_computation.5 | custom fusion | bytes 3147264 | tf_op jit(solution)/shard_map/gather | solution.py:84
  39.3 2.8 gather_fusion.4
  42.2 2.9 fusion
  45.1 24.7 %all-to-all-done = bf16[8,48,2048]{2,1,0:T(8,128)(2,1)} async-done(((bf16[8,48,2048]{2,1,0:T(8,128)(2,1)}), bf16[8,48,2048]{2,1,0:T(8,128)(2,1)}, u32[]{:S(2)}, u32[]{:S(2)}) %all-to-all-start) | async-done | bytes 1572896 | tf_op jit(solution)/shard_map/all_to_all | solution.py:41
  69.8 4.3 all-to-all-start.2
  74.4 5.0 fusion.22
  79.3 3.8 fusion.25
  83.1 29.2 %all-to-all-done.2 = bf16[8,48,2048]{2,1,0:T(8,128)(2,1)} async-done(((bf16[8,48,2048]{2,1,0:T(8,128)(2,1)}), bf16[8,48,2048]{2,1,0:T(8,128)(2,1)}, u32[]{:S(2)}, u32[]{:S(2)}) %all-to-all-start.2) | async-done | bytes 1572896 | tf_op jit(solution)/shard_map/all_to_all | solution.py:88
  112.4 3.7 multiply_convert_fusion.1
  116.1 3.9 fusion.15
  120.0 3.3 fusion.14
  123.3 3.2 fusion.13
  126.6 4.5 maximum_bitcast_fusion
  131.0 12.4 %copy.41 = bf16[2048,2304]{1,0:T(8,128)(2,1)} copy(bf16[2048,2304]{0,1:T(8,128)(2,1)} %maximum_bitcast_fusion) | data formatting | bytes 18874368
  143.4 3.7 fusion.18
  147.1 4.5 all-to-all-start.1
  151.7 3.8 fusion.5
  158.1 31.7 %all-to-all-done.1 = bf16[8,48,2048]{2,1,0:T(8,128)(2,1)} async-done(((bf16[8,48,2048]{2,1,0:T(8,128)(2,1)}), bf16[8,48,2048]{2,1,0:T(8,128)(2,1)}, u32[]{:S(2)}, u32[]{:S(2)}) %all-to-all-start.1) | async-done | bytes 1572896 | tf_op jit(solution)/shard_map/all_to_all | solution.py:54
  189.8 4.3 all-to-all-start.3
  197.0 4.3 gather_fusion.2
  201.3 3.9 gather_fusion.3
  205.2 27.1 %all-to-all-done.3 = bf16[8,48,2048]{2,1,0:T(8,128)(2,1)} async-done(((bf16[8,48,2048]{2,1,0:T(8,128)(2,1)}), bf16[8,48,2048]{2,1,0:T(8,128)(2,1)}, u32[]{:S(2)}, u32[]{:S(2)}) %all-to-all-start.3) | async-done | bytes 1572896 | tf_op jit(solution)/shard_map/all_to_all | solution.py:104
  235.1 3.9 gather_fusion.8
  239.0 3.9 gather_fusion.7
  242.9 3.9 gather_fusion.1
  246.8 3.9 gather_fusion.6
  250.6 3.0 fusion.38
  254.7 3.3 fusion.21
  266.6 227.7 %all-reduce.6.cloned.1.call-done = f32[2048,8]{0,1:T(8,128)} async-done(((f32[2048,8]{0,1:T(8,128)}), f32[2048,8]{0,1:T(8,128)}) %all-reduce.6.cloned.1.call-update) | async-done | bytes 65552 | tf_op jit(solution)/shard_map/psum | solution.py:143
  (60 shorter events, 26.5 us)
Async XLA Ops:
  8.0 104.4 %copy-start = (bf16[1,2048,768]{2,1,0:T(8,128)(2,1)S(1)}, bf16[1,2048,768]{2,1,0:T(8,128)(2,1)}, u32[]{:S(2)}) copy-start(bf16[1,2048,768]{2,1,0:T(8,128)(2,1)} %param.14) | copy-start | bytes 9437188
  20.3 49.5 %all-to-all-start = ((bf16[8,48,2048]{2,1,0:T(8,128)(2,1)}), bf16[8,48,2048]{2,1,0:T(8,128)(2,1)}, u32[]{:S(2)}, u32[]{:S(2)}) async-start(bf16[8,48,2048]{2,1,0:T(8,128)(2,1)} %bitcast.129), calls=%async_computation | async-start | bytes 3145728 | tf_op jit(solution)/shard_map/all_to_all | solution.py:41
  31.2 6.2 %copy-start.2 = (f32[2048,8]{0,1:T(8,128)S(1)}, f32[2048,8]{0,1:T(8,128)}, u32[]{:S(2)}) copy-start(f32[2048,8]{0,1:T(8,128)} %param.11) | copy-start | bytes 196612
  31.2 7.8 %copy-start.3 = (s32[128,3]{0,1:T(4,128)S(1)}, s32[128,3]{0,1:T(4,128)}, u32[]{:S(2)}) copy-start(s32[128,3]{0,1:T(4,128)} %param.9) | copy-start | bytes 4612
  31.2 7.8 %copy-start.4 = (s32[128,3]{0,1:T(4,128)S(1)}, s32[128,3]{0,1:T(4,128)}, u32[]{:S(2)}) copy-start(s32[128,3]{0,1:T(4,128)} %param.10) | copy-start | bytes 4612
  69.8 42.6 %all-to-all-start.2 = ((bf16[8,48,2048]{2,1,0:T(8,128)(2,1)}), bf16[8,48,2048]{2,1,0:T(8,128)(2,1)}, u32[]{:S(2)}, u32[]{:S(2)}) async-start(bf16[8,48,2048]{2,1,0:T(8,128)(2,1)} %fusion), calls=%async_computation.2 | async-start | bytes 3145728 | tf_op jit(solution)/shard_map/all_to_all | solution.py:88
  74.1 183.9 %reduce-scatter.4.cloned.1.call-start = ((), (), s32[]{:S(2)}) async-start(), calls=%async_computation.6 | async-start | bytes 9732096
  74.3 5.0 copy-start.5
  116.1 3.9 copy-start.10
  116.1 3.9 copy-start.9
  116.1 7.2 %copy-start.7 = (bf16[8,1,48,768]{3,2,0,1:T(8,128)(2,1)}, bf16[8,1,48,768]{3,2,0,1:T(8,128)(2,1)S(1)}, u32[]{:S(2)}) copy-start(bf16[8,1,48,768]{3,2,0,1:T(8,128)(2,1)S(1)} %get-tuple-element.11) | copy-start | bytes 1769476
  147.1 42.7 %all-to-all-start.1 = ((bf16[8,48,2048]{2,1,0:T(8,128)(2,1)}), bf16[8,48,2048]{2,1,0:T(8,128)(2,1)}, u32[]{:S(2)}, u32[]{:S(2)}) async-start(bf16[8,48,2048]{2,1,0:T(8,128)(2,1)} %fusion.18), calls=%async_computation.1 | async-start | bytes 3145728 | tf_op jit(solution)/shard_map/all_to_all | solution.py:54
  151.6 3.9 copy-start.6
  151.7 3.9 copy-start.8
  189.8 42.5 %all-to-all-start.3 = ((bf16[8,48,2048]{2,1,0:T(8,128)(2,1)}), bf16[8,48,2048]{2,1,0:T(8,128)(2,1)}, u32[]{:S(2)}, u32[]{:S(2)}) async-start(bf16[8,48,2048]{2,1,0:T(8,128)(2,1)} %add_convert_fusion), calls=%async_computation.3 | async-start | bytes 3145728 | tf_op jit(solution)/shard_map/all_to_all | solution.py:104
  194.1 300.2 %all-reduce.6.cloned.1.call-start = ((), (), s32[]{:S(2)}) async-start(), calls=%async_computation.5 | async-start | bytes 131072 | tf_op jit(solution)/shard_map/psum | solution.py:143
  250.6 3.1 copy-start.1
Sparse Core Ops, SparseCore 0:
  143.6 99.7 reduce-scatter.3
Sparse Core Ops, SparseCore 1:
  254.8 239.4 all-reduce.5
where the time goes:
time: 505 us; the launch traced here: 503 us
  waiting for transfers between devices  340 us (67%)
  local copies, waits for them, and re-layouts  74.4 us (15%)
  matrix products  38.8 us (8%)
  starting transfers between devices  22.4 us (4%)
  between operations  15.8 us (3%)
  other arithmetic  11.4 us (2%)
    psum x1, waiting for transfers between devices, on_device(): lax.psum(jnp.dot(tokens_wide.T, logit_grad, precision=highest), ('dp', 'e...  228 us
    all_to_all x1, waiting for transfers between devices, on_device(): lax.all_to_all(expert_out.reshape(sender_count * local_count, item_count,...  31.7 us
    all_to_all x1, waiting for transfers between devices, on_device(): lax.all_to_all(grad_rows, 'expert', split_axis=0, concat_axis=0, tiled=True)  29.2 us
    all_to_all x1, waiting for transfers between devices, on_device(): lax.all_to_all(row_grad.reshape(sender_count * local_count, slot_count, w...  27.1 us
    all_to_all x1, waiting for transfers between devices, on_device(): lax.all_to_all(outgoing, 'expert', split_axis=0, concat_axis=0, tiled=True)  24.7 us
    unnamed x28, local copies, waits for them, and re-layouts  20.4 us
    gather x3, local copies, waits for them, and re-layouts, on_device(): got_row = out_pad[position[:, which]].astype(jnp.float32)  12.1 us
    gather x3, local copies, waits for them, and re-layouts, on_device(): row_sum = row_sum + back_pad[position[:, which]].astype(jnp.float32)  11.7 us
  transfers between devices with their start and end apart: 6, of which 5 were waited for; matrix products, arithmetic and copies ran while one was open for 16% of the time, Pallas kernels for 0%

commit v1 on v0

--- a/solution.py
+++ b/solution.py
@@ -140,7 +140,10 @@
     grad_tokens = (row_sum + jnp.dot(logit_grad, w_router.T, precision=highest)).astype(
         jnp.bfloat16
     )
-    grad_router = lax.psum(jnp.dot(tokens_wide.T, logit_grad, precision=highest), ("dp", "expert"))
+    grad_router = jnp.sum(
+        lax.all_gather(jnp.dot(tokens_wide.T, logit_grad, precision=highest), ("dp", "expert")),
+        axis=0,
+    )
     return (layer_output, grad_tokens, grad_router, grad_gate, grad_up, grad_down)
 
 

time: 505 us -> 350 us (0.69)
  waiting for transfers between devices: 340 us -> 144 us
  blocking collectives: 0 us -> 43.9 us
  other arithmetic: 11.4 us -> 18.7 us
    psum x1 -> x0, waiting for transfers between devices: 228 us -> none  [on_device(): lax.psum(jnp.dot(tokens_wide.T, logit_grad, precision=highest), ('dp', 'e...]
    all_gather x0 -> x1, waiting for transfers between devices: none -> 49.5 us  [on_device(): lax.all_gather(jnp.dot(tokens_wide.T, logit_grad, precision=highest), ('d...]
    all_to_all x0 -> x1, blocking collectives: none -> 43.9 us  [on_device(): lax.all_to_all(row_grad.reshape(sender_count * local_count, slot_count, w...]
    all_to_all x1 -> x0, waiting for transfers between devices: 27.1 us -> none  [on_device(): lax.all_to_all(row_grad.reshape(sender_count * local_count, slot_count, w...]
    all_to_all x1, waiting for transfers between devices: 31.7 us -> 40.1 us  [on_device(): lax.all_to_all(expert_out.reshape(sender_count * local_count, item_count,...]
    reduce_sum x0 -> x1, other arithmetic: none -> 7.22 us  [on_device(): jnp.sum(lax.all_gather(jnp.dot(tokens_wide.T, logit_grad, precision=highe...]
    unnamed x28 -> x27, local copies, waits for them, and re-layouts: 20.4 us -> 19.2 us
  transfers between devices with their start and end apart: 6 -> 5, of which waited for: 5 -> 4; matrix products, arithmetic and copies ran while one was open for 16% -> 22% of each run, Pallas kernels for 0% -> 0%
where the time goes in v1:
time: 350 us; the launch traced here: 349 us
  waiting for transfers between devices  144 us (41%)
  local copies, waits for them, and re-layouts  71.2 us (20%)
  blocking collectives  43.9 us (13%)
  matrix products  37.5 us (11%)
  other arithmetic  18.7 us (5%)
  starting transfers between devices  18.2 us (5%)
  between operations  15.8 us (5%)
    all_gather x1, waiting for transfers between devices, on_device(): lax.all_gather(jnp.dot(tokens_wide.T, logit_grad, precision=highest), ('d...  49.5 us
    all_to_all x1, blocking collectives, on_device(): lax.all_to_all(row_grad.reshape(sender_count * local_count, slot_count, w...  43.9 us
    all_to_all x1, waiting for transfers between devices, on_device(): lax.all_to_all(expert_out.reshape(sender_count * local_count, item_count,...  40.1 us
    all_to_all x1, waiting for transfers between devices, on_device(): lax.all_to_all(grad_rows, 'expert', split_axis=0, concat_axis=0, tiled=True)  29.2 us
    all_to_all x1, waiting for transfers between devices, on_device(): lax.all_to_all(outgoing, 'expert', split_axis=0, concat_axis=0, tiled=True)  24.7 us
    unnamed x27, local copies, waits for them, and re-layouts  19.2 us
    gather x3, local copies, waits for them, and re-layouts, on_device(): got_row = out_pad[position[:, which]].astype(jnp.float32)  11.7 us
    gather x3, local copies, waits for them, and re-layouts, on_device(): row_sum = row_sum + back_pad[position[:, which]].astype(jnp.float32)  11.6 us
  transfers between devices with their start and end apart: 5, of which 4 were waited for; matrix products, arithmetic and copies ran while one was open for 22% of the time, Pallas kernels for 0%

profile of v1, /device:TPU:1, one launch (start us, length us, event | category | flops | bytes accessed | tf_op | source)
XLA Modules:
  0.0 348.9 jit_solution(3701645954325554006)
XLA Ops:
  9.2 2.9 scatter_custom_fusion
  14.1 6.2 %gather_fusion = bf16[384,2048]{1,0:T(8,128)(2,1)} fusion(bf16[129,2048]{1,0:T(8,128)(2,1)} %concatenate.23, s32[1024]{0:T(1024)S(1)} %get-tuple-element.27), kind=kCustom, calls=%fused_computation | custom fusion | bytes 3147264 | tf_op jit(solution)/shard_map/gather | solution.py:40
  20.3 9.1 %all-to-all-start = ((bf16[8,48,2048]{2,1,0:T(8,128)(2,1)}), bf16[8,48,2048]{2,1,0:T(8,128)(2,1)}, u32[]{:S(2)}, u32[]{:S(2)}) async-start(bf16[8,48,2048]{2,1,0:T(8,128)(2,1)} %bitcast.132), calls=%async_computation | async-start | bytes 3145728 | tf_op jit(solution)/shard_map/all_to_all | solution.py:41
  31.4 2.8 gather_fusion.4
  36.2 6.2 %gather_fusion.5 = bf16[384,2048]{1,0:T(8,128)(2,1)} fusion(bf16[129,2048]{1,0:T(8,128)(2,1)} %concatenate.26, s32[1024]{0:T(1024)S(1)} %get-tuple-element.27), kind=kCustom, calls=%fused_computation.5 | custom fusion | bytes 3147264 | tf_op jit(solution)/shard_map/gather | solution.py:84
  42.4 2.9 fusion
  45.2 24.7 %all-to-all-done = bf16[8,48,2048]{2,1,0:T(8,128)(2,1)} async-done(((bf16[8,48,2048]{2,1,0:T(8,128)(2,1)}), bf16[8,48,2048]{2,1,0:T(8,128)(2,1)}, u32[]{:S(2)}, u32[]{:S(2)}) %all-to-all-start) | async-done | bytes 1572896 | tf_op jit(solution)/shard_map/all_to_all | solution.py:41
  70.0 4.3 %all-to-all-start.2 = ((bf16[8,48,2048]{2,1,0:T(8,128)(2,1)}), bf16[8,48,2048]{2,1,0:T(8,128)(2,1)}, u32[]{:S(2)}, u32[]{:S(2)}) async-start(bf16[8,48,2048]{2,1,0:T(8,128)(2,1)} %fusion), calls=%async_computation.2 | async-start | bytes 3145728 | tf_op jit(solution)/shard_map/all_to_all | solution.py:88
  74.5 4.9 %fusion.22 = f32[8,1,48,768]{3,2,0,1:T(8,128)} fusion(bf16[8,48,2048]{2,1,0:T(8,128)(2,1)} %all-to-all-done, bf16[1,2048,768]{2,1,0:T(8,128)(2,1)} %param.12), kind=kOutput, calls=%fused_computation.39 | convolution fusion | flops 1207959552 | bytes 5898240 | tf_op jit(solution)/shard_map/slnd,ldf->slnf/dot_general | solution.py:44
  79.5 3.8 %fusion.25 = f32[8,1,48,768]{3,2,0,1:T(8,128)} fusion(bf16[8,48,2048]{2,1,0:T(8,128)(2,1)} %all-to-all-done, bf16[1,2048,768]{2,1,0:T(8,128)(2,1)S(1)} %copy-done.5), kind=kOutput, calls=%fused_computation.40 | convolution fusion | flops 1207959552 | bytes 5898240 | tf_op jit(solution)/shard_map/slnd,ldf->slnf/dot_general | solution.py:47
  83.3 29.2 %all-to-all-done.2 = bf16[8,48,2048]{2,1,0:T(8,128)(2,1)} async-done(((bf16[8,48,2048]{2,1,0:T(8,128)(2,1)}), bf16[8,48,2048]{2,1,0:T(8,128)(2,1)}, u32[]{:S(2)}, u32[]{:S(2)}) %all-to-all-start.2) | async-done | bytes 1572896 | tf_op jit(solution)/shard_map/all_to_all | solution.py:88
  112.5 3.7 %multiply_convert_fusion.1 = (bf16[8,1,48,768]{3,2,0,1:T(8,128)(2,1)S(1)}, bf16[8,48,768]{2,1,0:T(8,128)(2,1)S(1)}, bf16[8,48,768]{2,1,0:T(8,128)(2,1)S(1)}) fusion(f32[8,1,48,768]{3,2,0,1:T(8,128)} %fusion.22, f32[8,1,48,768]{3,2,0,1:T(8,128)} %fusion.25, bf16[8,48,2048]{2,1,0:T(8,128)(2,1)} %all-to-all-done.2, bf16[1,2048,768]{2,1,0:T(8,128)(2,1)S(1)} %copy-done), kind=kOutput, calls=%fused_computation.46 | convolution fusion | flops 1212383232 | bytes 8847360 | tf_op jit(solution)/shard_map/slnd,ldf->slnf/dot_general | solution.py:97
  116.3 3.9 %fusion.15 = bf16[2048,1,768]{0,2,1:T(8,128)(2,1)S(1)} fusion(bf16[8,48,768]{2,1,0:T(8,128)(2,1)S(1)} %get-tuple-element.13, bf16[8,48,2048]{2,1,0:T(8,128)(2,1)} %all-to-all-done.2), kind=kOutput, calls=%fused_computation.31 | convolution fusion | flops 1209532416 | bytes 5308416 | tf_op jit(solution)/shard_map/slnd,slnf->dlf/dot_general | solution.py:117
  120.2 3.2 fusion.13
  123.5 3.2 fusion.14
  126.7 4.5 %maximum_bitcast_fusion = bf16[2048,2304]{0,1:T(8,128)(2,1)} fusion(bf16[2048,1,768]{0,2,1:T(8,128)(2,1)S(1)} %fusion.15, bf16[2048,1,768]{0,2,1:T(8,128)(2,1)S(1)} %fusion.14, bf16[2048,1,768]{0,2,1:T(8,128)(2,1)S(1)} %fusion.13), kind=kLoop, calls=%fused_computation.10 | loop fusion | flops 28311552 | bytes 18874368 | tf_op jit(solution)/shard_map/convert_element_type | solution.py:124
  131.2 12.6 %copy.41 = bf16[2048,2304]{1,0:T(8,128)(2,1)} copy(bf16[2048,2304]{0,1:T(8,128)(2,1)} %maximum_bitcast_fusion) | data formatting | bytes 18874368
  143.9 3.6 %fusion.18 = bf16[8,48,2048]{2,1,0:T(8,128)(2,1)} fusion(bf16[8,48,768]{2,1,0:T(8,128)(2,1)} %copy-done.10, bf16[1,2048,768]{2,1,0:T(8,128)(2,1)S(1)} %copy-done), kind=kOutput, calls=%fused_computation.32 | convolution fusion | flops 1208745984 | bytes 5308416 | tf_op jit(solution)/shard_map/slnf,ldf->slnd/dot_general | solution.py:51
  147.5 4.3 %all-to-all-start.1 = ((bf16[8,48,2048]{2,1,0:T(8,128)(2,1)}), bf16[8,48,2048]{2,1,0:T(8,128)(2,1)}, u32[]{:S(2)}, u32[]{:S(2)}) async-start(bf16[8,48,2048]{2,1,0:T(8,128)(2,1)} %fusion.18), calls=%async_computation.1 | async-start | bytes 3145728 | tf_op jit(solution)/shard_map/all_to_all | solution.py:54
  152.2 40.1 %all-to-all-done.1 = bf16[8,48,2048]{2,1,0:T(8,128)(2,1)} async-done(((bf16[8,48,2048]{2,1,0:T(8,128)(2,1)}), bf16[8,48,2048]{2,1,0:T(8,128)(2,1)}, u32[]{:S(2)}, u32[]{:S(2)}) %all-to-all-start.1) | async-done | bytes 1572896 | tf_op jit(solution)/shard_map/all_to_all | solution.py:54
  195.1 3.9 %gather_fusion.2 = bf16[128,2048]{1,0:T(8,128)(2,1)} fusion(bf16[385,2048]{1,0:T(8,128)(2,1)} %concatenate.24, s32[1024]{0:T(1024)S(1)} %get-tuple-element.29), kind=kCustom, calls=%fused_computation.2 | custom fusion | bytes 1049088 | tf_op jit(solution)/shard_map/gather | solution.py:76
  198.9 3.9 %gather_fusion.3 = bf16[128,2048]{1,0:T(8,128)(2,1)} fusion(bf16[385,2048]{1,0:T(8,128)(2,1)} %concatenate.24, s32[1024]{0:T(1024)S(1)} %get-tuple-element.28), kind=kCustom, calls=%fused_computation.3 | custom fusion | bytes 1049088 | tf_op jit(solution)/shard_map/gather | solution.py:76
  202.8 3.9 %gather_fusion.1 = bf16[128,2048]{1,0:T(8,128)(2,1)} fusion(bf16[385,2048]{1,0:T(8,128)(2,1)} %concatenate.24, s32[1024]{0:T(1024)S(1)} %pad_clamp_fusion.3), kind=kCustom, calls=%fused_computation.1 | custom fusion | bytes 1049088 | tf_op jit(solution)/shard_map/gather | solution.py:76
  206.7 3.1 fusion.38
  210.9 3.7 %fusion.5 = f32[8,48,2048]{2,1,0:T(8,128)S(1)} fusion(bf16[8,48,768]{2,1,0:T(8,128)(2,1)} %copy-done.9, bf16[1,2048,768]{2,1,0:T(8,128)(2,1)} %param.13), kind=kOutput, calls=%fused_computation.20 | convolution fusion | flops 1207959552 | bytes 6881280 | tf_op jit(solution)/shard_map/slnf,ldf->slnd/dot_general | solution.py:102
  216.0 43.9 %all_to_all.20 = bf16[8,48,2048]{2,1,0:T(8,128)(2,1)S(1)} all-to-all(bf16[8,48,2048]{2,1,0:T(8,128)(2,1)S(1)} %add_convert_fusion), channel_id=1, replica_groups=mesh['dp'=32,'expert'=8] {'expert'}, dimensions={0} | all-to-all | bytes 3145728 | tf_op jit(solution)/shard_map/all_to_all | solution.py:104
  261.3 3.9 %gather_fusion.7 = bf16[128,2048]{1,0:T(8,128)(2,1)} fusion(bf16[385,2048]{1,0:T(8,128)(2,1)} %concatenate.27, s32[1024]{0:T(1024)S(1)} %get-tuple-element.29), kind=kCustom, calls=%fused_computation.7 | custom fusion | bytes 1049088 | tf_op jit(solution)/shard_map/gather | solution.py:136
  265.2 3.9 %gather_fusion.8 = bf16[128,2048]{1,0:T(8,128)(2,1)} fusion(bf16[385,2048]{1,0:T(8,128)(2,1)} %concatenate.27, s32[1024]{0:T(1024)S(1)} %get-tuple-element.28), kind=kCustom, calls=%fused_computation.8 | custom fusion | bytes 1049088 | tf_op jit(solution)/shard_map/gather | solution.py:136
  269.0 3.9 %gather_fusion.6 = bf16[128,2048]{1,0:T(8,128)(2,1)} fusion(bf16[385,2048]{1,0:T(8,128)(2,1)} %concatenate.27, s32[1024]{0:T(1024)S(1)} %pad_clamp_fusion.3), kind=kCustom, calls=%fused_computation.6 | custom fusion | bytes 1049088 | tf_op jit(solution)/shard_map/gather | solution.py:136
  272.9 3.3 fusion.21
  284.8 49.5 %all-gather.3.cloned.1.call-done = f32[524288,8]{0,1:T(8,128)} async-done(((f32[2048,8]{0,1:T(8,128)}), f32[524288,8]{0,1:T(8,128)}) %all-gather.3.cloned.1.call-update) | async-done | bytes 16777232 | tf_op jit(solution)/shard_map/all_gather | solution.py:144
  334.3 7.2 %reduce_sum.79 = f32[2048,8]{0,1:T(8,128)} reduce(f32[256,2048,8]{1,2,0:T(8,128)} %bitcast.130, f32[]{:T(128)} %constant.14.clone.1), dimensions={0}, to_apply=%region_8.9 | reduce | flops 4177920 | bytes 16842756 | tf_op jit(solution)/shard_map/reduce_sum | solution.py:143
  (59 shorter events, 22.7 us)
Async XLA Ops:
  8.0 104.5 %copy-start = (bf16[1,2048,768]{2,1,0:T(8,128)(2,1)S(1)}, bf16[1,2048,768]{2,1,0:T(8,128)(2,1)}, u32[]{:S(2)}) copy-start(bf16[1,2048,768]{2,1,0:T(8,128)(2,1)} %param.14) | copy-start | bytes 9437188
  20.3 9.2 %copy-start.2 = (f32[2048,8]{0,1:T(8,128)S(1)}, f32[2048,8]{0,1:T(8,128)}, u32[]{:S(2)}) copy-start(f32[2048,8]{0,1:T(8,128)} %param.11) | copy-start | bytes 196612
  20.3 10.7 %copy-start.3 = (s32[128,3]{0,1:T(4,128)S(1)}, s32[128,3]{0,1:T(4,128)}, u32[]{:S(2)}) copy-start(s32[128,3]{0,1:T(4,128)} %param.9) | copy-start | bytes 4612
  20.3 10.8 %copy-start.4 = (s32[128,3]{0,1:T(4,128)S(1)}, s32[128,3]{0,1:T(4,128)}, u32[]{:S(2)}) copy-start(s32[128,3]{0,1:T(4,128)} %param.10) | copy-start | bytes 4612
  20.3 49.7 %all-to-all-start = ((bf16[8,48,2048]{2,1,0:T(8,128)(2,1)}), bf16[8,48,2048]{2,1,0:T(8,128)(2,1)}, u32[]{:S(2)}, u32[]{:S(2)}) async-start(bf16[8,48,2048]{2,1,0:T(8,128)(2,1)} %bitcast.132), calls=%async_computation | async-start | bytes 3145728 | tf_op jit(solution)/shard_map/all_to_all | solution.py:41
  70.0 42.6 %all-to-all-start.2 = ((bf16[8,48,2048]{2,1,0:T(8,128)(2,1)}), bf16[8,48,2048]{2,1,0:T(8,128)(2,1)}, u32[]{:S(2)}, u32[]{:S(2)}) async-start(bf16[8,48,2048]{2,1,0:T(8,128)(2,1)} %fusion), calls=%async_computation.2 | async-start | bytes 3145728 | tf_op jit(solution)/shard_map/all_to_all | solution.py:88
  74.3 201.9 %reduce-scatter.4.cloned.1.call-start = ((), (), s32[]{:S(2)}) async-start(), calls=%async_computation.6 | async-start | bytes 9732096
  74.5 5.0 %copy-start.5 = (bf16[1,2048,768]{2,1,0:T(8,128)(2,1)S(1)}, bf16[1,2048,768]{2,1,0:T(8,128)(2,1)}, u32[]{:S(2)}) copy-start(bf16[1,2048,768]{2,1,0:T(8,128)(2,1)} %param.13) | copy-start | bytes 9437188
  116.3 3.9 %copy-start.10 = (bf16[8,48,768]{2,1,0:T(8,128)(2,1)}, bf16[8,48,768]{2,1,0:T(8,128)(2,1)S(1)}, u32[]{:S(2)}) copy-start(bf16[8,48,768]{2,1,0:T(8,128)(2,1)S(1)} %get-tuple-element.13) | copy-start | bytes 1769476
  116.3 3.9 %copy-start.7 = (bf16[8,1,48,768]{3,2,0,1:T(8,128)(2,1)}, bf16[8,1,48,768]{3,2,0,1:T(8,128)(2,1)S(1)}, u32[]{:S(2)}) copy-start(bf16[8,1,48,768]{3,2,0,1:T(8,128)(2,1)S(1)} %get-tuple-element.11) | copy-start | bytes 1769476
  116.3 7.2 %copy-start.9 = (bf16[8,48,768]{2,1,0:T(8,128)(2,1)}, bf16[8,48,768]{2,1,0:T(8,128)(2,1)S(1)}, u32[]{:S(2)}) copy-start(bf16[8,48,768]{2,1,0:T(8,128)(2,1)S(1)} %get-tuple-element.12) | copy-start | bytes 1769476
  147.5 44.7 %all-to-all-start.1 = ((bf16[8,48,2048]{2,1,0:T(8,128)(2,1)}), bf16[8,48,2048]{2,1,0:T(8,128)(2,1)}, u32[]{:S(2)}, u32[]{:S(2)}) async-start(bf16[8,48,2048]{2,1,0:T(8,128)(2,1)} %fusion.18), calls=%async_computation.1 | async-start | bytes 3145728 | tf_op jit(solution)/shard_map/all_to_all | solution.py:54
  151.9 182.4 %all-gather.3.cloned.1.call-start = ((), (), s32[]{:S(2)}) async-start(), calls=%async_computation.5 | async-start | bytes 16842752 | tf_op jit(solution)/shard_map/all_gather | solution.py:144
  206.7 3.1 copy-start.1
  210.8 3.8 %copy-start.6 = (bf16[1,2048,768]{2,1,0:T(8,128)(2,1)S(1)}, bf16[1,2048,768]{2,1,0:T(8,128)(2,1)}, u32[]{:S(2)}) copy-start(bf16[1,2048,768]{2,1,0:T(8,128)(2,1)} %param.12) | copy-start | bytes 9437188
  210.8 3.8 %copy-start.8 = (bf16[8,1,48,768]{3,2,0,1:T(8,128)(2,1)S(1)}, bf16[8,1,48,768]{3,2,0,1:T(8,128)(2,1)}, u32[]{:S(2)}) copy-start(bf16[8,1,48,768]{3,2,0,1:T(8,128)(2,1)} %copy-done.7) | copy-start | bytes 1769476
Sparse Core Ops, SparseCore 0:
  144.0 100.0 reduce-scatter.3
Sparse Core Ops, SparseCore 1:
  210.9 123.3 all-gather.2
